TPU v7x, 256 devices: a whole 4x4x8 slice. The times are simulated.
256 devices in a mesh: shell: 4 (over x_lo, core), tile: 64 (over z, x_hi, y).
Axes of the slice: x: 4 (x_hi: 2, x_lo: 2; x = x_hi * 2 + x_lo), y: 4, z: 8, core: 2. Of those that a mesh axis runs over, the one named last changes fastest.
Arguments:
- latent: float32 [64, 2048, 512], P('shell', 'tile'), may hold values from -5 to 5
- shell_sigma: float32 [64], P('shell'), may hold values from 0.15 to 0.6
- lens_weight: float32 [5, 64], P(None, 'shell'), may hold values from 0 to 0.5
- shear_kernel: bfloat16 [2, 33, 33], replicated, may hold values from -0.1875 to 0.1875
- star_mask: int32 [2048, 512], P('tile', 'shell'), may hold values 0 or 1
- gal_pix: int32 [16, 4096, 128], P('shell', 'tile'), may hold values from 0 to 4095
- gal_bin: int32 [16, 4096, 128], P('shell', 'tile'), may hold values from 0 to 4
- gal_shape: float32 [2, 16, 4096, 128], P(None, 'shell', 'tile'), may hold values from -3 to 3
- gal_weight: float32 [16, 4096, 128], P('shell', 'tile'), may hold values from 0.5 to 4
- gal_counts: int32 [16, 4096], P('shell', 'tile'), may hold values from 0 to 128, as said below
Outputs:
- grad_field: float32 [64, 2048, 512], P('shell', 'tile')
Inputs may be any that keep to these rules, and one draw needn't show every extreme that they name: Bucket (i, j) of the galaxy arrays holds galaxies for the tile j mod 64 and the column block i mod 4, in its first gal_counts[i, j] slots; in every draw some destination block receives 128 galaxies from every device, and buckets' loads range from near zero to 128.
All inputs are finite; a program needn't handle non-finite values. No bound on the sum of `star_mask` on one device may be relied on, other than what follows from the above.
Results may differ from a plain program's by a relative error of at most 0.0023.
Values may be sent and summed in bfloat16 or wider, within the bound.
No kernel may reach another device: no remote copies, remote signals or barrier semaphores. Data moves between devices by JAX's collectives and lax.ppermute only.
A program may use at most 64 MiB of HBM per device.

v0:
```python
import jax
import jax.numpy as jnp
from jax import lax
from jax.sharding import PartitionSpec as P

NBIN = 5
KER = 33
HALF = 16


def extended(block, sides, width):
    for axis, dim in sides:
        count = lax.axis_size(axis)
        forward = [(i, i + 1) for i in range(count - 1)]
        backward = [(target, source) for source, target in forward]
        low = lax.ppermute(
            lax.slice_in_dim(block, block.shape[dim] - width, None, axis=dim), axis, forward
        )
        high = lax.ppermute(lax.slice_in_dim(block, 0, width, axis=dim), axis, backward)
        block = jnp.concatenate([low, block, high], axis=dim)
    return block


def build_bands(kernel, columns):
    span = columns + KER - 1
    grid_shape = (KER, span, columns)
    lagged = lax.broadcasted_iota(jnp.int32, grid_shape, 1) - lax.broadcasted_iota(
        jnp.int32, grid_shape, 2
    )
    onehot = (lagged == lax.broadcasted_iota(jnp.int32, grid_shape, 0)).astype(jnp.bfloat16)
    bands = jnp.einsum("kdv,vjc->kdjc", kernel, onehot, preferred_element_type=jnp.float32)
    return bands.astype(jnp.bfloat16)


def stacked_rows(padded, height):
    return jnp.stack([padded[..., offset : offset + height, :] for offset in range(KER)], axis=-3)


def deposit_block(shear_rows, codes, observed, weights, columns):
    row_count = shear_rows.shape[1]
    usable = codes >= 0
    safe_codes = jnp.where(usable, codes, 0)
    row_of = safe_codes // columns
    col_of = safe_codes % columns
    rows_hot = (
        row_of[:, None] == lax.broadcasted_iota(jnp.int32, (codes.shape[0], row_count), 1)
    ).astype(jnp.float32)
    cols_hot = (
        col_of[:, None] == lax.broadcasted_iota(jnp.int32, (codes.shape[0], columns), 1)
    ).astype(jnp.float32)
    picked = jnp.einsum(
        "gr,krc->kgc",
        rows_hot,
        shear_rows,
        precision=lax.Precision.HIGHEST,
        preferred_element_type=jnp.float32,
    )
    predicted = jnp.sum(picked * cols_hot[None], axis=2)
    scaled = jnp.where(usable, weights, 0.0)
    residual = scaled[None] * (predicted - observed)
    spread = residual[:, :, None] * cols_hot[None]
    return jnp.einsum(
        "gr,kgc->krc",
        rows_hot,
        spread,
        precision=lax.Precision.HIGHEST,
        preferred_element_type=jnp.float32,
    )


def per_device(
    latent,
    shell_sigma,
    lens_weight,
    shear_kernel,
    star_mask,
    gal_pix,
    gal_bin,
    gal_shape,
    gal_weight,
    gal_counts,
):
    height = latent.shape[1]
    width = latent.shape[2]
    shell_count = lax.axis_size("shell")
    columns = width // shell_count
    pixels = height * columns
    sigma = shell_sigma[:, None, None]
    growth = jnp.exp(sigma * latent - 0.5 * sigma * sigma)
    partial_bins = jnp.einsum(
        "bs,srw->brw",
        lens_weight,
        growth - 1.0,
        precision=lax.Precision.HIGHEST,
        preferred_element_type=jnp.float32,
    )
    bin_map = lax.psum_scatter(partial_bins, "shell", scatter_dimension=2, tiled=True).astype(
        jnp.bfloat16
    )
    padded = extended(bin_map, (("shell", 2), ("tile", 1)), HALF)
    forward_bands = build_bands(shear_kernel, columns)
    shear = jnp.einsum(
        "bdrj,kdjc->kbrc",
        stacked_rows(padded, height),
        forward_bands,
        preferred_element_type=jnp.float32,
    )
    slot_index = lax.broadcasted_iota(jnp.int32, gal_pix.shape, 2)
    codes = jnp.where(slot_index < gal_counts[:, :, None], gal_bin * pixels + gal_pix, -1).astype(
        jnp.float32
    )
    packet = jnp.concatenate([codes[None], gal_shape, gal_weight[None]], axis=0)
    arrived = lax.all_to_all(
        lax.all_to_all(packet, "shell", split_axis=1, concat_axis=1, tiled=True),
        "tile",
        split_axis=2,
        concat_axis=2,
        tiled=True,
    )
    shear_rows = shear.reshape(2, NBIN * height, columns)
    groups = arrived.shape[1]

    def add_group(group, total):
        block = lax.dynamic_index_in_dim(arrived, group, 1, keepdims=False).reshape(4, -1)
        group_codes = block[0].astype(jnp.int32)
        return total + deposit_block(shear_rows, group_codes, block[1:3], block[3], columns)

    summed = lax.fori_loop(0, groups, add_group, jnp.zeros_like(shear_rows))
    shear_grad = summed.reshape(2, NBIN, height, columns)
    masked = (shear_grad * star_mask.astype(jnp.float32)).astype(jnp.bfloat16)
    rims = extended(masked, (("shell", 3), ("tile", 2)), HALF)
    back_bands = build_bands(jnp.flip(shear_kernel, (1, 2)), columns)
    bin_grad = jnp.einsum(
        "kbdrj,kdjc->brc",
        stacked_rows(rims, height),
        back_bands,
        preferred_element_type=jnp.float32,
    )
    full_grad = lax.all_gather(bin_grad, "shell", axis=2, tiled=True)
    mixed = jnp.einsum(
        "bs,brw->srw",
        lens_weight,
        full_grad,
        precision=lax.Precision.HIGHEST,
        preferred_element_type=jnp.float32,
    )
    return sigma * growth * mixed


def solution(mesh):
    return jax.shard_map(
        per_device,
        mesh=mesh,
        in_specs=(
            P("shell", "tile", None),
            P("shell"),
            P(None, "shell"),
            P(),
            P("tile", "shell"),
            P("shell", "tile", None),
            P("shell", "tile", None),
            P(None, "shell", "tile", None),
            P("shell", "tile", None),
            P("shell", "tile"),
        ),
        out_specs=P("shell", "tile", None),
        check_vma=False,
    )
```

profile of v0, /device:TPU:31, one launch (start us, length us, event | category | flops | bytes accessed | tf_op | source)
XLA Modules:
  0.0 210.8 jit_solution(7721434345518271787)
XLA Ops:
  7.2 3.4 %convolution_bitcast_fusion.1 = f32[5,32,512]{2,0,1:T(8,128)} fusion(f32[16,32,512]{2,1,0:T(8,128)} %param.12, f32[16]{0:T(128)S(1)} %multiply_multiply_fusion, f32[16]{0:T(128)} %param.13, f32[5,16]{1,0:T(8,128)S(1)} %copy-done), kind=kOutput, calls=%fused_computation.44 | convolution fusion | flops 16515072 | bytes 1376704 | tf_op jit(solution)/shard_map/bs,srw->brw/dot_general | solution.py:90
  10.6 1.2 copy.26
  11.8 1.1 select_convert_fusion
  12.8 21.4 %reduce-scatter.2.cloned.1.call-done = f32[5,32,128]{2,0,1:T(8,128)} async-done(((f32[5,32,512]{2,0,1:T(8,128)}), f32[5,32,128]{2,0,1:T(8,128)}) %reduce-scatter.2.cloned.1.call-update) | async-done | bytes 81936 | tf_op jit(solution)/shard_map/reduce_scatter | solution.py:97
  35.2 1.3 collective-permute-start
  36.5 3.0 %collective-permute-start.1 = (bf16[5,32,16]{2,0,1:T(8,128)(2,1)S(1)}, bf16[5,32,16]{2,0,1:T(8,128)(2,1)S(1)}, u32[]{:S(2)}, u32[]{:S(2)}) collective-permute-start(bf16[5,32,16]{2,0,1:T(8,128)(2,1)S(1)} %get-tuple-element.165), channel_id=1, source_target_pairs={{64,0},{128,64},{192,128},{65,1},{129,65},{193,129},{66,2},{130,66... | collective-permute-start | bytes 15368 | tf_op jit(solution)/shard_map/ppermute | solution.py:19
  39.6 2.1 pad_maximum_fusion
  41.7 4.2 %all-to-all-start = ((f32[4,4,64,128]{3,0,2,1:T(4,128)}), f32[4,4,64,128]{3,0,2,1:T(4,128)}, u32[]{:S(2)}, u32[]{:S(2)}) async-start(f32[4,4,64,128]{3,0,2,1:T(4,128)} %pad_maximum_fusion), calls=%async_computation | async-start | bytes 1048576 | tf_op jit(solution)/shard_map/all_to_all | solution.py:114
  46.7 4.0 %collective-permute-start.2 = (bf16[5,16,160]{2,0,1:T(8,128)(2,1)}, bf16[5,16,160]{2,0,1:T(8,128)(2,1)}, u32[]{:S(2)}, u32[]{:S(2)}) collective-permute-start(bf16[5,16,160]{2,0,1:T(8,128)(2,1)} %get-tuple-element.161), channel_id=1, source_target_pairs={{0,1},{1,2},{2,3},{3,4},{4,5},{5,6},{6,7},{7,8},{8,9},{9,10},{10,1... | collective-permute-start | bytes 76808 | tf_op jit(solution)/shard_map/ppermute | solution.py:16
  50.7 1.9 collective-permute-start.3
  52.7 1.0 convert_bitcast_fusion.1
  53.7 1.9 copy.27
  55.6 13.7 %all-to-all-start.1 = ((f32[4,4,64,128]{3,0,1,2:T(4,128)}), f32[4,4,64,128]{3,0,1,2:T(4,128)}, u32[]{:S(2)}, u32[]{:S(2)}) async-start(f32[4,4,64,128]{3,0,1,2:T(4,128)} %copy.27), calls=%async_computation.1 | async-start | bytes 1048576 | tf_op jit(solution)/shard_map/all_to_all | solution.py:113
  69.3 1.0 pad_maximum_fusion.2
  71.1 1.6 fusion.34
  72.8 11.5 %all-to-all-done.1 = f32[4,4,64,128]{3,0,1,2:T(4,128)} async-done(((f32[4,4,64,128]{3,0,1,2:T(4,128)}), f32[4,4,64,128]{3,0,1,2:T(4,128)}, u32[]{:S(2)}, u32[]{:S(2)}) %all-to-all-start.1) | async-done | bytes 524320 | tf_op jit(solution)/shard_map/all_to_all | solution.py:113
  84.3 79.2 %while.16 = (s32[]{:T(128)}, f32[2,160,128]{2,1,0:T(8,128)}, f32[4,4,64,128]{3,0,1,2:T(4,128)}, f32[2,160,128]{2,1,0:T(8,128)S(1)}, s32[]{:T(128)}, /*index=5*/s32[]{:T(128)}, s32[]{}, s32[]{}) while((s32[]{:T(128)}, f32[2,160,128]{2,1,0:T(8,128)}, f32[4,4,64,128]{3,0,1,2:T(4,128)}, f32[2,160,128]{2,1,0:T(8,128)S(1)}, s32[]{:T(128)}, ...), condition=%wide.region_3.4_spmd.clone, body=%wide.region_1.3_spmd.clone.sunk | while | flops 8064376832 | bytes 40337624 | solution.py:128
  84.3 1.0 constant_dynamic-slice_fusion.3
  85.8 4.4 %fusion.112 = f32[8192,2]{0,1:T(2,128)S(1)} fusion(f32[8192,128]{0,1:T(8,128)S(1)} %fusion.111, f32[2,160,128]{2,1,0:T(8,128)S(1)} %get-tuple-element.218, s32[8192]{0:T(1024)S(1)} %get-tuple-element.196), kind=kOutput, calls=%fused_computation.11.clone.1 | convolution fusion | flops 4032020480 | bytes 4456448 | tf_op jit(solution)/shard_map/while/body/eval_jaxpr/gr,krc->kgc/dot_general | solution.py:51
  90.3 1.0 fusion.113
  91.3 5.6 %copy.80 = f32[8192,128]{1,0:T(8,128)} copy(f32[8192,128]{0,1:T(8,128)} %copy-done.1) | data formatting | bytes 8388608 | tf_op jit(solution)/shard_map/while/body/eval_jaxpr/convert_element_type | solution.py:50
  96.9 6.6 %fusion.114 = f32[2,160,128]{2,1,0:T(8,128)S(1)} fusion(s32[8192]{0:T(1024)S(1)} %get-tuple-element.196, f32[8192,128]{1,0:T(8,128)} %copy.80, f32[2,8192]{1,0:T(2,128)S(1)} %fusion.113, f32[2,160,128]{2,1,0:T(8,128)S(1)} %copy-done.3, pred[]{:T(512)S(6)} %compare.19), kind=kOutput, calls=%fused_computation.13.clone.1 | convolution fusion | flops 4030021632 | bytes 4620289 | tf_op jit(solution)/shard_map/while/body/eval_jaxpr/gr,kgc->krc/dot_general | solution.py:62
  104.1 1.1 constant_dynamic-slice_fusion.3
  105.6 4.4 %fusion.112 = f32[8192,2]{0,1:T(2,128)S(1)} fusion(f32[8192,128]{0,1:T(8,128)S(1)} %fusion.111, f32[2,160,128]{2,1,0:T(8,128)S(1)} %get-tuple-element.218, s32[8192]{0:T(1024)S(1)} %get-tuple-element.196), kind=kOutput, calls=%fused_computation.11.clone.1 | convolution fusion | flops 4032020480 | bytes 4456448 | tf_op jit(solution)/shard_map/while/body/eval_jaxpr/gr,krc->kgc/dot_general | solution.py:51
  110.1 1.0 fusion.113
  111.1 5.6 %copy.80 = f32[8192,128]{1,0:T(8,128)} copy(f32[8192,128]{0,1:T(8,128)} %copy-done.1) | data formatting | bytes 8388608 | tf_op jit(solution)/shard_map/while/body/eval_jaxpr/convert_element_type | solution.py:50
  116.7 6.6 %fusion.114 = f32[2,160,128]{2,1,0:T(8,128)S(1)} fusion(s32[8192]{0:T(1024)S(1)} %get-tuple-element.196, f32[8192,128]{1,0:T(8,128)} %copy.80, f32[2,8192]{1,0:T(2,128)S(1)} %fusion.113, f32[2,160,128]{2,1,0:T(8,128)S(1)} %copy-done.3, pred[]{:T(512)S(6)} %compare.19), kind=kOutput, calls=%fused_computation.13.clone.1 | convolution fusion | flops 4030021632 | bytes 4620289 | tf_op jit(solution)/shard_map/while/body/eval_jaxpr/gr,kgc->krc/dot_general | solution.py:62
  123.9 1.0 constant_dynamic-slice_fusion.3
  125.4 4.4 %fusion.112 = f32[8192,2]{0,1:T(2,128)S(1)} fusion(f32[8192,128]{0,1:T(8,128)S(1)} %fusion.111, f32[2,160,128]{2,1,0:T(8,128)S(1)} %get-tuple-element.218, s32[8192]{0:T(1024)S(1)} %get-tuple-element.196), kind=kOutput, calls=%fused_computation.11.clone.1 | convolution fusion | flops 4032020480 | bytes 4456448 | tf_op jit(solution)/shard_map/while/body/eval_jaxpr/gr,krc->kgc/dot_general | solution.py:51
  129.9 1.0 fusion.113
  130.9 5.6 %copy.80 = f32[8192,128]{1,0:T(8,128)} copy(f32[8192,128]{0,1:T(8,128)} %copy-done.1) | data formatting | bytes 8388608 | tf_op jit(solution)/shard_map/while/body/eval_jaxpr/convert_element_type | solution.py:50
  136.5 6.6 %fusion.114 = f32[2,160,128]{2,1,0:T(8,128)S(1)} fusion(s32[8192]{0:T(1024)S(1)} %get-tuple-element.196, f32[8192,128]{1,0:T(8,128)} %copy.80, f32[2,8192]{1,0:T(2,128)S(1)} %fusion.113, f32[2,160,128]{2,1,0:T(8,128)S(1)} %copy-done.3, pred[]{:T(512)S(6)} %compare.19), kind=kOutput, calls=%fused_computation.13.clone.1 | convolution fusion | flops 4030021632 | bytes 4620289 | tf_op jit(solution)/shard_map/while/body/eval_jaxpr/gr,kgc->krc/dot_general | solution.py:62
  143.7 1.0 constant_dynamic-slice_fusion.3
  145.2 4.4 %fusion.112 = f32[8192,2]{0,1:T(2,128)S(1)} fusion(f32[8192,128]{0,1:T(8,128)S(1)} %fusion.111, f32[2,160,128]{2,1,0:T(8,128)S(1)} %get-tuple-element.218, s32[8192]{0:T(1024)S(1)} %get-tuple-element.196), kind=kOutput, calls=%fused_computation.11.clone.1 | convolution fusion | flops 4032020480 | bytes 4456448 | tf_op jit(solution)/shard_map/while/body/eval_jaxpr/gr,krc->kgc/dot_general | solution.py:51
  149.7 1.0 fusion.113
  150.7 5.6 %copy.80 = f32[8192,128]{1,0:T(8,128)} copy(f32[8192,128]{0,1:T(8,128)} %copy-done.1) | data formatting | bytes 8388608 | tf_op jit(solution)/shard_map/while/body/eval_jaxpr/convert_element_type | solution.py:50
  156.3 6.6 %fusion.114 = f32[2,160,128]{2,1,0:T(8,128)S(1)} fusion(s32[8192]{0:T(1024)S(1)} %get-tuple-element.196, f32[8192,128]{1,0:T(8,128)} %copy.80, f32[2,8192]{1,0:T(2,128)S(1)} %fusion.113, f32[2,160,128]{2,1,0:T(8,128)S(1)} %copy-done.3, pred[]{:T(512)S(6)} %compare.19), kind=kOutput, calls=%fused_computation.13.clone.1 | convolution fusion | flops 4030021632 | bytes 4620289 | tf_op jit(solution)/shard_map/while/body/eval_jaxpr/gr,kgc->krc/dot_general | solution.py:62
  163.5 0.9 multiply_convert_fusion
  164.5 1.3 collective-permute-start.4
  165.8 5.4 %collective-permute-start.5 = (bf16[2,5,32,16]{3,2,1,0:T(8,128)(2,1)S(1)}, bf16[2,5,32,16]{3,2,1,0:T(8,128)(2,1)S(1)}, u32[]{:S(2)}, u32[]{:S(2)}) collective-permute-start(bf16[2,5,32,16]{3,2,1,0:T(8,128)(2,1)S(1)} %get-tuple-element.163), channel_id=1, source_target_pairs={{64,0},{128,64},{192,128},{65,1},{129,65},{193,129},{66,2},{130,66... | collective-permute-start | bytes 30728 | tf_op jit(solution)/shard_map/ppermute | solution.py:19
  172.3 5.0 %collective-permute-start.6 = (bf16[2,5,16,160]{3,2,1,0:T(8,128)(2,1)S(1)}, bf16[2,5,16,160]{3,2,1,0:T(8,128)(2,1)S(1)}, u32[]{:S(2)}, u32[]{:S(2)}) collective-permute-start(bf16[2,5,16,160]{3,2,1,0:T(8,128)(2,1)S(1)} %get-tuple-element.159), channel_id=1, source_target_pairs={{0,1},{1,2},{2,3},{3,4},{4,5},{5,6},{6,7},{7,8},{8,9},{9,10},{10,1... | collective-permute-start | bytes 153608 | tf_op jit(solution)/shard_map/ppermute | solution.py:16
  177.3 2.1 %collective-permute-start.7 = (bf16[2,5,16,160]{3,2,1,0:T(8,128)(2,1)S(1)}, bf16[2,5,16,160]{3,2,1,0:T(8,128)(2,1)S(1)}, u32[]{:S(2)}, u32[]{:S(2)}) collective-permute-start(bf16[2,5,16,160]{3,2,1,0:T(8,128)(2,1)S(1)} %get-tuple-element.158), channel_id=1, source_target_pairs={{1,0},{2,1},{3,2},{4,3},{5,4},{6,5},{7,6},{8,7},{9,8},{10,9},{11,1... | collective-permute-start | bytes 153608 | tf_op jit(solution)/shard_map/ppermute | solution.py:19
  179.5 1.0 convert_bitcast_fusion
  180.5 6.5 %collective-permute-done.7 = bf16[2,5,16,160]{3,2,1,0:T(8,128)(2,1)S(1)} collective-permute-done((bf16[2,5,16,160]{3,2,1,0:T(8,128)(2,1)S(1)}, bf16[2,5,16,160]{3,2,1,0:T(8,128)(2,1)S(1)}, u32[]{:S(2)}, u32[]{:S(2)}) %collective-permute-start.7) | collective-permute-done | bytes 51232 | tf_op jit(solution)/shard_map/ppermute | solution.py:19
  189.0 1.6 fusion.43
  190.6 10.1 %all_gather.3 = f32[5,32,512]{2,1,0:T(8,128)S(1)} all-gather(f32[5,32,128]{2,1,0:T(8,128)S(1)} %fusion.43), channel_id=1, replica_groups=mesh['shell'=4,'tile'=64] {'shell'}, dimensions={2}, use_global_device_ids=true | all-gather | bytes 409600 | tf_op jit(solution)/shard_map/all_gather | solution.py:139
  200.7 1.7 fusion.42
  202.3 1.6 copy.35
  (134 shorter events, 10.3 us)
Async XLA Ops:
  6.5 0.7 copy-start
  6.5 46.1 %copy-start.5 = (bf16[2,33,33]{2,0,1:T(2,128)(2,1)S(1)}, bf16[2,33,33]{2,0,1:T(2,128)(2,1)}, u32[]{:S(2)}) copy-start(bf16[2,33,33]{2,0,1:T(2,128)(2,1)} %param.15) | copy-start | bytes 13072
  6.5 27.7 %reduce-scatter.2.cloned.1.call-start = ((), (), s32[]{:S(2)}) async-start(), calls=%async_computation.3 | async-start | bytes 655360 | tf_op jit(solution)/shard_map/reduce_scatter | solution.py:97
  10.6 43.1 %copy-start.6 = (s32[32,128]{1,0:T(8,128)S(1)}, s32[32,128]{1,0:T(8,128)}, u32[]{:S(2)}) copy-start(s32[32,128]{1,0:T(8,128)} %param.16) | copy-start | bytes 49156
  35.2 10.7 %collective-permute-start = (bf16[5,32,16]{2,0,1:T(8,128)(2,1)S(1)}, bf16[5,32,16]{2,0,1:T(8,128)(2,1)S(1)}, u32[]{:S(2)}, u32[]{:S(2)}) collective-permute-start(bf16[5,32,16]{2,0,1:T(8,128)(2,1)S(1)} %get-tuple-element.164), channel_id=1, source_target_pairs={{0,64},{64,128},{128,192},{1,65},{65,129},{129,193},{2,66},{66,130... | collective-permute-start | bytes 15368 | tf_op jit(solution)/shard_map/ppermute | solution.py:16
  36.5 9.4 %collective-permute-start.1 = (bf16[5,32,16]{2,0,1:T(8,128)(2,1)S(1)}, bf16[5,32,16]{2,0,1:T(8,128)(2,1)S(1)}, u32[]{:S(2)}, u32[]{:S(2)}) collective-permute-start(bf16[5,32,16]{2,0,1:T(8,128)(2,1)S(1)} %get-tuple-element.165), channel_id=1, source_target_pairs={{64,0},{128,64},{192,128},{65,1},{129,65},{193,129},{66,2},{130,66... | collective-permute-start | bytes 15368 | tf_op jit(solution)/shard_map/ppermute | solution.py:19
  41.7 12.1 %all-to-all-start = ((f32[4,4,64,128]{3,0,2,1:T(4,128)}), f32[4,4,64,128]{3,0,2,1:T(4,128)}, u32[]{:S(2)}, u32[]{:S(2)}) async-start(f32[4,4,64,128]{3,0,2,1:T(4,128)} %pad_maximum_fusion), calls=%async_computation | async-start | bytes 1048576 | tf_op jit(solution)/shard_map/all_to_all | solution.py:114
  46.7 22.6 %collective-permute-start.2 = (bf16[5,16,160]{2,0,1:T(8,128)(2,1)}, bf16[5,16,160]{2,0,1:T(8,128)(2,1)}, u32[]{:S(2)}, u32[]{:S(2)}) collective-permute-start(bf16[5,16,160]{2,0,1:T(8,128)(2,1)} %get-tuple-element.161), channel_id=1, source_target_pairs={{0,1},{1,2},{2,3},{3,4},{4,5},{5,6},{6,7},{7,8},{8,9},{9,10},{10,1... | collective-permute-start | bytes 76808 | tf_op jit(solution)/shard_map/ppermute | solution.py:16
  50.7 18.6 %collective-permute-start.3 = (bf16[5,16,160]{2,0,1:T(8,128)(2,1)}, bf16[5,16,160]{2,0,1:T(8,128)(2,1)}, u32[]{:S(2)}, u32[]{:S(2)}) collective-permute-start(bf16[5,16,160]{2,0,1:T(8,128)(2,1)} %get-tuple-element.160), channel_id=1, source_target_pairs={{1,0},{2,1},{3,2},{4,3},{5,4},{6,5},{7,6},{8,7},{9,8},{10,9},{11,1... | collective-permute-start | bytes 76808 | tf_op jit(solution)/shard_map/ppermute | solution.py:19
  55.6 28.6 %all-to-all-start.1 = ((f32[4,4,64,128]{3,0,1,2:T(4,128)}), f32[4,4,64,128]{3,0,1,2:T(4,128)}, u32[]{:S(2)}, u32[]{:S(2)}) async-start(f32[4,4,64,128]{3,0,1,2:T(4,128)} %copy.27), calls=%async_computation.1 | async-start | bytes 1048576 | tf_op jit(solution)/shard_map/all_to_all | solution.py:113
  85.8 4.4 %copy-start.1 = (f32[8192,128]{0,1:T(8,128)}, f32[8192,128]{0,1:T(8,128)S(1)}, u32[]{:S(2)}) copy-start(f32[8192,128]{0,1:T(8,128)S(1)} %fusion.111) | copy-start | bytes 12582916 | tf_op jit(solution)/shard_map/while
  90.3 6.6 %copy-start.3 = (f32[2,160,128]{2,1,0:T(8,128)S(1)}, f32[2,160,128]{2,1,0:T(8,128)}, u32[]{:S(2)}) copy-start(f32[2,160,128]{2,1,0:T(8,128)} %get-tuple-element.208) | copy-start | bytes 491524 | tf_op jit(solution)/shard_map/while
  103.4 0.7 copy-start.4
  105.6 4.4 %copy-start.1 = (f32[8192,128]{0,1:T(8,128)}, f32[8192,128]{0,1:T(8,128)S(1)}, u32[]{:S(2)}) copy-start(f32[8192,128]{0,1:T(8,128)S(1)} %fusion.111) | copy-start | bytes 12582916 | tf_op jit(solution)/shard_map/while
  110.1 6.6 %copy-start.3 = (f32[2,160,128]{2,1,0:T(8,128)S(1)}, f32[2,160,128]{2,1,0:T(8,128)}, u32[]{:S(2)}) copy-start(f32[2,160,128]{2,1,0:T(8,128)} %get-tuple-element.208) | copy-start | bytes 491524 | tf_op jit(solution)/shard_map/while
  123.2 0.7 copy-start.4
  125.4 4.4 %copy-start.1 = (f32[8192,128]{0,1:T(8,128)}, f32[8192,128]{0,1:T(8,128)S(1)}, u32[]{:S(2)}) copy-start(f32[8192,128]{0,1:T(8,128)S(1)} %fusion.111) | copy-start | bytes 12582916 | tf_op jit(solution)/shard_map/while
  129.9 6.6 %copy-start.3 = (f32[2,160,128]{2,1,0:T(8,128)S(1)}, f32[2,160,128]{2,1,0:T(8,128)}, u32[]{:S(2)}) copy-start(f32[2,160,128]{2,1,0:T(8,128)} %get-tuple-element.208) | copy-start | bytes 491524 | tf_op jit(solution)/shard_map/while
  143.0 0.7 copy-start.4
  145.2 4.4 %copy-start.1 = (f32[8192,128]{0,1:T(8,128)}, f32[8192,128]{0,1:T(8,128)S(1)}, u32[]{:S(2)}) copy-start(f32[8192,128]{0,1:T(8,128)S(1)} %fusion.111) | copy-start | bytes 12582916 | tf_op jit(solution)/shard_map/while
  149.7 6.6 %copy-start.3 = (f32[2,160,128]{2,1,0:T(8,128)S(1)}, f32[2,160,128]{2,1,0:T(8,128)}, u32[]{:S(2)}) copy-start(f32[2,160,128]{2,1,0:T(8,128)} %get-tuple-element.208) | copy-start | bytes 491524 | tf_op jit(solution)/shard_map/while
  162.8 0.7 copy-start.4
  164.5 6.9 %collective-permute-start.4 = (bf16[2,5,32,16]{3,2,1,0:T(8,128)(2,1)S(1)}, bf16[2,5,32,16]{3,2,1,0:T(8,128)(2,1)S(1)}, u32[]{:S(2)}, u32[]{:S(2)}) collective-permute-start(bf16[2,5,32,16]{3,2,1,0:T(8,128)(2,1)S(1)} %get-tuple-element.162), channel_id=1, source_target_pairs={{0,64},{64,128},{128,192},{1,65},{65,129},{129,193},{2,66},{66,130... | collective-permute-start | bytes 30728 | tf_op jit(solution)/shard_map/ppermute | solution.py:16
  165.8 6.3 %collective-permute-start.5 = (bf16[2,5,32,16]{3,2,1,0:T(8,128)(2,1)S(1)}, bf16[2,5,32,16]{3,2,1,0:T(8,128)(2,1)S(1)}, u32[]{:S(2)}, u32[]{:S(2)}) collective-permute-start(bf16[2,5,32,16]{3,2,1,0:T(8,128)(2,1)S(1)} %get-tuple-element.163), channel_id=1, source_target_pairs={{64,0},{128,64},{192,128},{65,1},{129,65},{193,129},{66,2},{130,66... | collective-permute-start | bytes 30728 | tf_op jit(solution)/shard_map/ppermute | solution.py:19
  172.3 8.2 %collective-permute-start.6 = (bf16[2,5,16,160]{3,2,1,0:T(8,128)(2,1)S(1)}, bf16[2,5,16,160]{3,2,1,0:T(8,128)(2,1)S(1)}, u32[]{:S(2)}, u32[]{:S(2)}) collective-permute-start(bf16[2,5,16,160]{3,2,1,0:T(8,128)(2,1)S(1)} %get-tuple-element.159), channel_id=1, source_target_pairs={{0,1},{1,2},{2,3},{3,4},{4,5},{5,6},{6,7},{7,8},{8,9},{9,10},{10,1... | collective-permute-start | bytes 153608 | tf_op jit(solution)/shard_map/ppermute | solution.py:16
  177.3 9.7 %collective-permute-start.7 = (bf16[2,5,16,160]{3,2,1,0:T(8,128)(2,1)S(1)}, bf16[2,5,16,160]{3,2,1,0:T(8,128)(2,1)S(1)}, u32[]{:S(2)}, u32[]{:S(2)}) collective-permute-start(bf16[2,5,16,160]{3,2,1,0:T(8,128)(2,1)S(1)} %get-tuple-element.158), channel_id=1, source_target_pairs={{1,0},{2,1},{3,2},{4,3},{5,4},{6,5},{7,6},{8,7},{9,8},{10,9},{11,1... | collective-permute-start | bytes 153608 | tf_op jit(solution)/shard_map/ppermute | solution.py:19
  189.0 11.7 %copy-start.2 = (f32[16,32,512]{2,1,0:T(8,128)S(1)}, f32[16,32,512]{2,1,0:T(8,128)}, u32[]{:S(2)}) copy-start(f32[16,32,512]{2,1,0:T(8,128)} %param.12) | copy-start | bytes 3145732
  189.0 11.7 %copy-start.7 = (f32[16]{0:T(128)S(1)}, f32[16]{0:T(128)}, u32[]{:S(2)}) copy-start(f32[16]{0:T(128)} %param.13) | copy-start | bytes 196
Sparse Core Ops, SparseCore 0:
  10.7 23.4 reduce-scatter.1
where the time goes:
time: 212 us; the launch traced here: 211 us
  matrix products  54 us (25%)
  starting transfers between devices  42 us (20%)
  waiting for transfers between devices  40.2 us (19%)
  local copies, waits for them, and re-layouts  36.5 us (17%)
  between operations  14.2 us (7%)
  other arithmetic  13.4 us (6%)
  blocking collectives  10.1 us (5%)
    dot_general x4, matrix products, deposit_block(): jnp.einsum('gr,kgc->krc', rows_hot, spread, precision=lax.Precision.HIGHE...  26.2 us
    convert_element_type x4, local copies, waits for them, and re-layouts, deposit_block(): cols_hot = (col_of[:, None] == lax.broadcasted_iota(jnp.int32, (codes.sha...  22.3 us
    reduce_scatter x1, waiting for transfers between devices, per_device(): lax.psum_scatter(partial_bins, 'shell', scatter_dimension=2, tiled=True)  21.4 us
    dot_general x4, matrix products, deposit_block(): jnp.einsum('gr,krc->kgc', rows_hot, shear_rows, precision=lax.Precision.H...  17.6 us
    all_to_all x1, starting transfers between devices, per_device(): lax.all_to_all(lax.all_to_all(packet, 'shell', split_axis=1, concat_axis=...  13.7 us
    ppermute x4, starting transfers between devices, extended(): lax.ppermute(lax.slice_in_dim(block, 0, width, axis=dim), axis, backward)  12.5 us
    ppermute x4, starting transfers between devices, extended(): lax.ppermute(lax.slice_in_dim(block, block.shape[dim] - width, None, axis...  11.6 us
    all_to_all x1, waiting for transfers between devices, per_device(): lax.all_to_all(lax.all_to_all(packet, 'shell', split_axis=1, concat_axis=...  11.5 us
  transfers between devices with their start and end apart: 11, of which 4 were waited for; matrix products, arithmetic and copies ran while one was open for 6% of the time, Pallas kernels for 0%

commit v1 on v0

--- a/solution.py
+++ b/solution.py
@@ -136,7 +136,9 @@
         back_bands,
         preferred_element_type=jnp.float32,
     )
-    full_grad = lax.all_gather(bin_grad, "shell", axis=2, tiled=True)
+    full_grad = jnp.concatenate(
+        lax.all_to_all(jnp.stack([bin_grad] * lax.axis_size("shell")), "shell", 0, 0), axis=2
+    )
     mixed = jnp.einsum(
         "bs,brw->srw",
         lens_weight,

time: 212 us -> 215 us (1.014)
    all_to_all x0 -> x1, blocking collectives: none -> 11.6 us  [per_device(): lax.all_to_all(jnp.stack([bin_grad] * lax.axis_size('shell')), 'shell', 0...]
    all_gather x1 -> x0, blocking collectives: 10.1 us -> none  [per_device(): full_grad = lax.all_gather(bin_grad, 'shell', axis=2, tiled=True)]
where the time goes in v1:
time: 215 us; the launch traced here: 213 us
  matrix products  54 us (25%)
  starting transfers between devices  42 us (20%)
  waiting for transfers between devices  40.2 us (19%)
  local copies, waits for them, and re-layouts  36.8 us (17%)
  between operations  14.2 us (7%)
  other arithmetic  13.4 us (6%)
  blocking collectives  11.6 us (5%)
    dot_general x4, matrix products, deposit_block(): jnp.einsum('gr,kgc->krc', rows_hot, spread, precision=lax.Precision.HIGHE...  26.2 us
    convert_element_type x4, local copies, waits for them, and re-layouts, deposit_block(): cols_hot = (col_of[:, None] == lax.broadcasted_iota(jnp.int32, (codes.sha...  22.3 us
    reduce_scatter x1, waiting for transfers between devices, per_device(): lax.psum_scatter(partial_bins, 'shell', scatter_dimension=2, tiled=True)  21.4 us
    dot_general x4, matrix products, deposit_block(): jnp.einsum('gr,krc->kgc', rows_hot, shear_rows, precision=lax.Precision.H...  17.6 us
    all_to_all x1, starting transfers between devices, per_device(): lax.all_to_all(lax.all_to_all(packet, 'shell', split_axis=1, concat_axis=...  13.7 us
    ppermute x4, starting transfers between devices, extended(): lax.ppermute(lax.slice_in_dim(block, 0, width, axis=dim), axis, backward)  12.5 us
    all_to_all x1, blocking collectives, per_device(): lax.all_to_all(jnp.stack([bin_grad] * lax.axis_size('shell')), 'shell', 0...  11.6 us
    ppermute x4, starting transfers between devices, extended(): lax.ppermute(lax.slice_in_dim(block, block.shape[dim] - width, None, axis...  11.6 us
  transfers between devices with their start and end apart: 11, of which 4 were waited for; matrix products, arithmetic and copies ran while one was open for 6% of the time, Pallas kernels for 0%

profile of v1, /device:TPU:31, one launch (start us, length us, event | category | flops | bytes accessed | tf_op | source)
XLA Modules:
  0.0 212.6 jit_solution(13942366559168624233)
XLA Ops:
  7.2 3.4 %convolution_bitcast_fusion.1 = f32[5,32,512]{2,0,1:T(8,128)} fusion(f32[16,32,512]{2,1,0:T(8,128)} %param.12, f32[16]{0:T(128)S(1)} %multiply_multiply_fusion, f32[16]{0:T(128)} %param.13, f32[5,16]{1,0:T(8,128)S(1)} %copy-done), kind=kOutput, calls=%fused_computation.44 | convolution fusion | flops 16515072 | bytes 1376704 | tf_op jit(solution)/shard_map/bs,srw->brw/dot_general | solution.py:90
  10.6 1.2 copy.105
  11.8 1.1 select_convert_fusion
  12.8 21.4 %reduce-scatter.2.cloned.1.call-done = f32[5,32,128]{2,0,1:T(8,128)} async-done(((f32[5,32,512]{2,0,1:T(8,128)}), f32[5,32,128]{2,0,1:T(8,128)}) %reduce-scatter.2.cloned.1.call-update) | async-done | bytes 81936 | tf_op jit(solution)/shard_map/reduce_scatter | solution.py:97
  35.2 1.3 collective-permute-start
  36.5 3.0 %collective-permute-start.1 = (bf16[5,32,16]{2,0,1:T(8,128)(2,1)S(1)}, bf16[5,32,16]{2,0,1:T(8,128)(2,1)S(1)}, u32[]{:S(2)}, u32[]{:S(2)}) collective-permute-start(bf16[5,32,16]{2,0,1:T(8,128)(2,1)S(1)} %get-tuple-element.165), channel_id=1, source_target_pairs={{64,0},{128,64},{192,128},{65,1},{129,65},{193,129},{66,2},{130,66... | collective-permute-start | bytes 15368 | tf_op jit(solution)/shard_map/ppermute | solution.py:19
  39.6 2.1 pad_maximum_fusion
  41.7 4.2 %all-to-all-start = ((f32[4,4,64,128]{3,0,2,1:T(4,128)}), f32[4,4,64,128]{3,0,2,1:T(4,128)}, u32[]{:S(2)}, u32[]{:S(2)}) async-start(f32[4,4,64,128]{3,0,2,1:T(4,128)} %pad_maximum_fusion), calls=%async_computation | async-start | bytes 1048576 | tf_op jit(solution)/shard_map/all_to_all | solution.py:114
  46.7 4.0 %collective-permute-start.2 = (bf16[5,16,160]{2,0,1:T(8,128)(2,1)}, bf16[5,16,160]{2,0,1:T(8,128)(2,1)}, u32[]{:S(2)}, u32[]{:S(2)}) collective-permute-start(bf16[5,16,160]{2,0,1:T(8,128)(2,1)} %get-tuple-element.161), channel_id=1, source_target_pairs={{0,1},{1,2},{2,3},{3,4},{4,5},{5,6},{6,7},{7,8},{8,9},{9,10},{10,1... | collective-permute-start | bytes 76808 | tf_op jit(solution)/shard_map/ppermute | solution.py:16
  50.7 1.9 collective-permute-start.3
  52.7 1.0 convert_bitcast_fusion.1
  53.7 1.9 copy.106
  55.6 13.7 %all-to-all-start.1 = ((f32[4,4,64,128]{3,0,1,2:T(4,128)}), f32[4,4,64,128]{3,0,1,2:T(4,128)}, u32[]{:S(2)}, u32[]{:S(2)}) async-start(f32[4,4,64,128]{3,0,1,2:T(4,128)} %copy.106), calls=%async_computation.1 | async-start | bytes 1048576 | tf_op jit(solution)/shard_map/all_to_all | solution.py:113
  69.3 1.0 pad_maximum_fusion.2
  71.1 1.6 fusion.34
  72.8 11.5 %all-to-all-done.1 = f32[4,4,64,128]{3,0,1,2:T(4,128)} async-done(((f32[4,4,64,128]{3,0,1,2:T(4,128)}), f32[4,4,64,128]{3,0,1,2:T(4,128)}, u32[]{:S(2)}, u32[]{:S(2)}) %all-to-all-start.1) | async-done | bytes 524320 | tf_op jit(solution)/shard_map/all_to_all | solution.py:113
  84.3 79.2 %while.16 = (s32[]{:T(128)}, f32[2,160,128]{2,1,0:T(8,128)}, f32[4,4,64,128]{3,0,1,2:T(4,128)}, f32[2,160,128]{2,1,0:T(8,128)S(1)}, s32[]{:T(128)}, /*index=5*/s32[]{:T(128)}, s32[]{}, s32[]{}) while((s32[]{:T(128)}, f32[2,160,128]{2,1,0:T(8,128)}, f32[4,4,64,128]{3,0,1,2:T(4,128)}, f32[2,160,128]{2,1,0:T(8,128)S(1)}, s32[]{:T(128)}, ...), condition=%wide.region_3.4_spmd.clone, body=%wide.region_1.3_spmd.clone.sunk | while | flops 8064376832 | bytes 40337624 | solution.py:128
  84.3 1.0 constant_dynamic-slice_fusion.3
  85.8 4.4 %fusion.113 = f32[8192,2]{0,1:T(2,128)S(1)} fusion(f32[8192,128]{0,1:T(8,128)S(1)} %fusion.112, f32[2,160,128]{2,1,0:T(8,128)S(1)} %get-tuple-element.218, s32[8192]{0:T(1024)S(1)} %get-tuple-element.196), kind=kOutput, calls=%fused_computation.11.clone.1 | convolution fusion | flops 4032020480 | bytes 4456448 | tf_op jit(solution)/shard_map/while/body/eval_jaxpr/gr,krc->kgc/dot_general | solution.py:51
  90.3 1.0 fusion.114
  91.3 5.6 %copy.164 = f32[8192,128]{1,0:T(8,128)} copy(f32[8192,128]{0,1:T(8,128)} %copy-done.1) | data formatting | bytes 8388608 | tf_op jit(solution)/shard_map/while/body/eval_jaxpr/convert_element_type | solution.py:50
  96.9 6.6 %fusion.115 = f32[2,160,128]{2,1,0:T(8,128)S(1)} fusion(s32[8192]{0:T(1024)S(1)} %get-tuple-element.196, f32[8192,128]{1,0:T(8,128)} %copy.164, f32[2,8192]{1,0:T(2,128)S(1)} %fusion.114, f32[2,160,128]{2,1,0:T(8,128)S(1)} %copy-done.3, pred[]{:T(512)S(6)} %compare.19), kind=kOutput, calls=%fused_computation.13.clone.1 | convolution fusion | flops 4030021632 | bytes 4620289 | tf_op jit(solution)/shard_map/while/body/eval_jaxpr/gr,kgc->krc/dot_general | solution.py:62
  104.1 1.1 constant_dynamic-slice_fusion.3
  105.6 4.4 %fusion.113 = f32[8192,2]{0,1:T(2,128)S(1)} fusion(f32[8192,128]{0,1:T(8,128)S(1)} %fusion.112, f32[2,160,128]{2,1,0:T(8,128)S(1)} %get-tuple-element.218, s32[8192]{0:T(1024)S(1)} %get-tuple-element.196), kind=kOutput, calls=%fused_computation.11.clone.1 | convolution fusion | flops 4032020480 | bytes 4456448 | tf_op jit(solution)/shard_map/while/body/eval_jaxpr/gr,krc->kgc/dot_general | solution.py:51
  110.1 1.0 fusion.114
  111.1 5.6 %copy.164 = f32[8192,128]{1,0:T(8,128)} copy(f32[8192,128]{0,1:T(8,128)} %copy-done.1) | data formatting | bytes 8388608 | tf_op jit(solution)/shard_map/while/body/eval_jaxpr/convert_element_type | solution.py:50
  116.7 6.6 %fusion.115 = f32[2,160,128]{2,1,0:T(8,128)S(1)} fusion(s32[8192]{0:T(1024)S(1)} %get-tuple-element.196, f32[8192,128]{1,0:T(8,128)} %copy.164, f32[2,8192]{1,0:T(2,128)S(1)} %fusion.114, f32[2,160,128]{2,1,0:T(8,128)S(1)} %copy-done.3, pred[]{:T(512)S(6)} %compare.19), kind=kOutput, calls=%fused_computation.13.clone.1 | convolution fusion | flops 4030021632 | bytes 4620289 | tf_op jit(solution)/shard_map/while/body/eval_jaxpr/gr,kgc->krc/dot_general | solution.py:62
  123.9 1.0 constant_dynamic-slice_fusion.3
  125.4 4.4 %fusion.113 = f32[8192,2]{0,1:T(2,128)S(1)} fusion(f32[8192,128]{0,1:T(8,128)S(1)} %fusion.112, f32[2,160,128]{2,1,0:T(8,128)S(1)} %get-tuple-element.218, s32[8192]{0:T(1024)S(1)} %get-tuple-element.196), kind=kOutput, calls=%fused_computation.11.clone.1 | convolution fusion | flops 4032020480 | bytes 4456448 | tf_op jit(solution)/shard_map/while/body/eval_jaxpr/gr,krc->kgc/dot_general | solution.py:51
  129.9 1.0 fusion.114
  130.9 5.6 %copy.164 = f32[8192,128]{1,0:T(8,128)} copy(f32[8192,128]{0,1:T(8,128)} %copy-done.1) | data formatting | bytes 8388608 | tf_op jit(solution)/shard_map/while/body/eval_jaxpr/convert_element_type | solution.py:50
  136.5 6.6 %fusion.115 = f32[2,160,128]{2,1,0:T(8,128)S(1)} fusion(s32[8192]{0:T(1024)S(1)} %get-tuple-element.196, f32[8192,128]{1,0:T(8,128)} %copy.164, f32[2,8192]{1,0:T(2,128)S(1)} %fusion.114, f32[2,160,128]{2,1,0:T(8,128)S(1)} %copy-done.3, pred[]{:T(512)S(6)} %compare.19), kind=kOutput, calls=%fused_computation.13.clone.1 | convolution fusion | flops 4030021632 | bytes 4620289 | tf_op jit(solution)/shard_map/while/body/eval_jaxpr/gr,kgc->krc/dot_general | solution.py:62
  143.7 1.0 constant_dynamic-slice_fusion.3
  145.2 4.4 %fusion.113 = f32[8192,2]{0,1:T(2,128)S(1)} fusion(f32[8192,128]{0,1:T(8,128)S(1)} %fusion.112, f32[2,160,128]{2,1,0:T(8,128)S(1)} %get-tuple-element.218, s32[8192]{0:T(1024)S(1)} %get-tuple-element.196), kind=kOutput, calls=%fused_computation.11.clone.1 | convolution fusion | flops 4032020480 | bytes 4456448 | tf_op jit(solution)/shard_map/while/body/eval_jaxpr/gr,krc->kgc/dot_general | solution.py:51
  149.7 1.0 fusion.114
  150.7 5.6 %copy.164 = f32[8192,128]{1,0:T(8,128)} copy(f32[8192,128]{0,1:T(8,128)} %copy-done.1) | data formatting | bytes 8388608 | tf_op jit(solution)/shard_map/while/body/eval_jaxpr/convert_element_type | solution.py:50
  156.3 6.6 %fusion.115 = f32[2,160,128]{2,1,0:T(8,128)S(1)} fusion(s32[8192]{0:T(1024)S(1)} %get-tuple-element.196, f32[8192,128]{1,0:T(8,128)} %copy.164, f32[2,8192]{1,0:T(2,128)S(1)} %fusion.114, f32[2,160,128]{2,1,0:T(8,128)S(1)} %copy-done.3, pred[]{:T(512)S(6)} %compare.19), kind=kOutput, calls=%fused_computation.13.clone.1 | convolution fusion | flops 4030021632 | bytes 4620289 | tf_op jit(solution)/shard_map/while/body/eval_jaxpr/gr,kgc->krc/dot_general | solution.py:62
  163.5 0.9 fusion.85
  164.5 1.3 collective-permute-start.4
  165.8 5.4 %collective-permute-start.5 = (bf16[2,5,32,16]{3,2,0,1:T(8,128)(2,1)S(1)}, bf16[2,5,32,16]{3,2,0,1:T(8,128)(2,1)S(1)}, u32[]{:S(2)}, u32[]{:S(2)}) collective-permute-start(bf16[2,5,32,16]{3,2,0,1:T(8,128)(2,1)S(1)} %get-tuple-element.163), channel_id=1, source_target_pairs={{64,0},{128,64},{192,128},{65,1},{129,65},{193,129},{66,2},{130,66... | collective-permute-start | bytes 30728 | tf_op jit(solution)/shard_map/ppermute | solution.py:19
  172.3 5.0 %collective-permute-start.6 = (bf16[2,5,16,160]{3,2,0,1:T(8,128)(2,1)S(1)}, bf16[2,5,16,160]{3,2,0,1:T(8,128)(2,1)S(1)}, u32[]{:S(2)}, u32[]{:S(2)}) collective-permute-start(bf16[2,5,16,160]{3,2,0,1:T(8,128)(2,1)S(1)} %get-tuple-element.159), channel_id=1, source_target_pairs={{0,1},{1,2},{2,3},{3,4},{4,5},{5,6},{6,7},{7,8},{8,9},{9,10},{10,1... | collective-permute-start | bytes 153608 | tf_op jit(solution)/shard_map/ppermute | solution.py:16
  177.3 2.1 %collective-permute-start.7 = (bf16[2,5,16,160]{3,2,0,1:T(8,128)(2,1)S(1)}, bf16[2,5,16,160]{3,2,0,1:T(8,128)(2,1)S(1)}, u32[]{:S(2)}, u32[]{:S(2)}) collective-permute-start(bf16[2,5,16,160]{3,2,0,1:T(8,128)(2,1)S(1)} %get-tuple-element.158), channel_id=1, source_target_pairs={{1,0},{2,1},{3,2},{4,3},{5,4},{6,5},{7,6},{8,7},{9,8},{10,9},{11,1... | collective-permute-start | bytes 153608 | tf_op jit(solution)/shard_map/ppermute | solution.py:19
  179.5 1.0 convert_bitcast_fusion
  180.5 6.5 %collective-permute-done.7 = bf16[2,5,16,160]{3,2,0,1:T(8,128)(2,1)S(1)} collective-permute-done((bf16[2,5,16,160]{3,2,0,1:T(8,128)(2,1)S(1)}, bf16[2,5,16,160]{3,2,0,1:T(8,128)(2,1)S(1)}, u32[]{:S(2)}, u32[]{:S(2)}) %collective-permute-start.7) | collective-permute-done | bytes 51232 | tf_op jit(solution)/shard_map/ppermute | solution.py:19
  189.0 1.6 fusion.43
  190.6 11.6 %all_to_all.15 = f32[4,5,32,128]{3,2,1,0:T(8,128)S(1)} all-to-all(f32[4,5,32,128]{3,2,1,0:T(8,128)S(1)} %stack.279), channel_id=1, replica_groups=mesh['shell'=4,'tile'=64] {'shell'}, dimensions={0} | all-to-all | bytes 655360 | tf_op jit(solution)/shard_map/all_to_all | solution.py:140
  202.6 1.6 fusion.42
  204.2 1.6 copy.116
  (137 shorter events, 10.7 us)
Async XLA Ops:
  6.5 0.7 copy-start
  6.5 46.1 %copy-start.5 = (bf16[2,33,33]{2,0,1:T(2,128)(2,1)S(1)}, bf16[2,33,33]{2,0,1:T(2,128)(2,1)}, u32[]{:S(2)}) copy-start(bf16[2,33,33]{2,0,1:T(2,128)(2,1)} %param.15) | copy-start | bytes 13072
  6.5 27.7 %reduce-scatter.2.cloned.1.call-start = ((), (), s32[]{:S(2)}) async-start(), calls=%async_computation.4 | async-start | bytes 655360 | tf_op jit(solution)/shard_map/reduce_scatter | solution.py:97
  10.6 43.1 %copy-start.6 = (s32[32,128]{1,0:T(8,128)S(1)}, s32[32,128]{1,0:T(8,128)}, u32[]{:S(2)}) copy-start(s32[32,128]{1,0:T(8,128)} %param.16) | copy-start | bytes 49156
  35.2 10.7 %collective-permute-start = (bf16[5,32,16]{2,0,1:T(8,128)(2,1)S(1)}, bf16[5,32,16]{2,0,1:T(8,128)(2,1)S(1)}, u32[]{:S(2)}, u32[]{:S(2)}) collective-permute-start(bf16[5,32,16]{2,0,1:T(8,128)(2,1)S(1)} %get-tuple-element.164), channel_id=1, source_target_pairs={{0,64},{64,128},{128,192},{1,65},{65,129},{129,193},{2,66},{66,130... | collective-permute-start | bytes 15368 | tf_op jit(solution)/shard_map/ppermute | solution.py:16
  36.5 9.4 %collective-permute-start.1 = (bf16[5,32,16]{2,0,1:T(8,128)(2,1)S(1)}, bf16[5,32,16]{2,0,1:T(8,128)(2,1)S(1)}, u32[]{:S(2)}, u32[]{:S(2)}) collective-permute-start(bf16[5,32,16]{2,0,1:T(8,128)(2,1)S(1)} %get-tuple-element.165), channel_id=1, source_target_pairs={{64,0},{128,64},{192,128},{65,1},{129,65},{193,129},{66,2},{130,66... | collective-permute-start | bytes 15368 | tf_op jit(solution)/shard_map/ppermute | solution.py:19
  41.7 12.1 %all-to-all-start = ((f32[4,4,64,128]{3,0,2,1:T(4,128)}), f32[4,4,64,128]{3,0,2,1:T(4,128)}, u32[]{:S(2)}, u32[]{:S(2)}) async-start(f32[4,4,64,128]{3,0,2,1:T(4,128)} %pad_maximum_fusion), calls=%async_computation | async-start | bytes 1048576 | tf_op jit(solution)/shard_map/all_to_all | solution.py:114
  46.7 22.6 %collective-permute-start.2 = (bf16[5,16,160]{2,0,1:T(8,128)(2,1)}, bf16[5,16,160]{2,0,1:T(8,128)(2,1)}, u32[]{:S(2)}, u32[]{:S(2)}) collective-permute-start(bf16[5,16,160]{2,0,1:T(8,128)(2,1)} %get-tuple-element.161), channel_id=1, source_target_pairs={{0,1},{1,2},{2,3},{3,4},{4,5},{5,6},{6,7},{7,8},{8,9},{9,10},{10,1... | collective-permute-start | bytes 76808 | tf_op jit(solution)/shard_map/ppermute | solution.py:16
  50.7 18.6 %collective-permute-start.3 = (bf16[5,16,160]{2,0,1:T(8,128)(2,1)}, bf16[5,16,160]{2,0,1:T(8,128)(2,1)}, u32[]{:S(2)}, u32[]{:S(2)}) collective-permute-start(bf16[5,16,160]{2,0,1:T(8,128)(2,1)} %get-tuple-element.160), channel_id=1, source_target_pairs={{1,0},{2,1},{3,2},{4,3},{5,4},{6,5},{7,6},{8,7},{9,8},{10,9},{11,1... | collective-permute-start | bytes 76808 | tf_op jit(solution)/shard_map/ppermute | solution.py:19
  55.6 28.6 %all-to-all-start.1 = ((f32[4,4,64,128]{3,0,1,2:T(4,128)}), f32[4,4,64,128]{3,0,1,2:T(4,128)}, u32[]{:S(2)}, u32[]{:S(2)}) async-start(f32[4,4,64,128]{3,0,1,2:T(4,128)} %copy.106), calls=%async_computation.1 | async-start | bytes 1048576 | tf_op jit(solution)/shard_map/all_to_all | solution.py:113
  85.8 4.4 %copy-start.1 = (f32[8192,128]{0,1:T(8,128)}, f32[8192,128]{0,1:T(8,128)S(1)}, u32[]{:S(2)}) copy-start(f32[8192,128]{0,1:T(8,128)S(1)} %fusion.112) | copy-start | bytes 12582916 | tf_op jit(solution)/shard_map/while
  90.3 6.6 %copy-start.3 = (f32[2,160,128]{2,1,0:T(8,128)S(1)}, f32[2,160,128]{2,1,0:T(8,128)}, u32[]{:S(2)}) copy-start(f32[2,160,128]{2,1,0:T(8,128)} %get-tuple-element.208) | copy-start | bytes 491524 | tf_op jit(solution)/shard_map/while
  103.4 0.7 copy-start.4
  105.6 4.4 %copy-start.1 = (f32[8192,128]{0,1:T(8,128)}, f32[8192,128]{0,1:T(8,128)S(1)}, u32[]{:S(2)}) copy-start(f32[8192,128]{0,1:T(8,128)S(1)} %fusion.112) | copy-start | bytes 12582916 | tf_op jit(solution)/shard_map/while
  110.1 6.6 %copy-start.3 = (f32[2,160,128]{2,1,0:T(8,128)S(1)}, f32[2,160,128]{2,1,0:T(8,128)}, u32[]{:S(2)}) copy-start(f32[2,160,128]{2,1,0:T(8,128)} %get-tuple-element.208) | copy-start | bytes 491524 | tf_op jit(solution)/shard_map/while
  123.2 0.7 copy-start.4
  125.4 4.4 %copy-start.1 = (f32[8192,128]{0,1:T(8,128)}, f32[8192,128]{0,1:T(8,128)S(1)}, u32[]{:S(2)}) copy-start(f32[8192,128]{0,1:T(8,128)S(1)} %fusion.112) | copy-start | bytes 12582916 | tf_op jit(solution)/shard_map/while
  129.9 6.6 %copy-start.3 = (f32[2,160,128]{2,1,0:T(8,128)S(1)}, f32[2,160,128]{2,1,0:T(8,128)}, u32[]{:S(2)}) copy-start(f32[2,160,128]{2,1,0:T(8,128)} %get-tuple-element.208) | copy-start | bytes 491524 | tf_op jit(solution)/shard_map/while
  143.0 0.7 copy-start.4
  145.2 4.4 %copy-start.1 = (f32[8192,128]{0,1:T(8,128)}, f32[8192,128]{0,1:T(8,128)S(1)}, u32[]{:S(2)}) copy-start(f32[8192,128]{0,1:T(8,128)S(1)} %fusion.112) | copy-start | bytes 12582916 | tf_op jit(solution)/shard_map/while
  149.7 6.6 %copy-start.3 = (f32[2,160,128]{2,1,0:T(8,128)S(1)}, f32[2,160,128]{2,1,0:T(8,128)}, u32[]{:S(2)}) copy-start(f32[2,160,128]{2,1,0:T(8,128)} %get-tuple-element.208) | copy-start | bytes 491524 | tf_op jit(solution)/shard_map/while
  162.8 0.7 copy-start.4
  164.5 6.9 %collective-permute-start.4 = (bf16[2,5,32,16]{3,2,0,1:T(8,128)(2,1)S(1)}, bf16[2,5,32,16]{3,2,0,1:T(8,128)(2,1)S(1)}, u32[]{:S(2)}, u32[]{:S(2)}) collective-permute-start(bf16[2,5,32,16]{3,2,0,1:T(8,128)(2,1)S(1)} %get-tuple-element.162), channel_id=1, source_target_pairs={{0,64},{64,128},{128,192},{1,65},{65,129},{129,193},{2,66},{66,130... | collective-permute-start | bytes 30728 | tf_op jit(solution)/shard_map/ppermute | solution.py:16
  165.8 6.3 %collective-permute-start.5 = (bf16[2,5,32,16]{3,2,0,1:T(8,128)(2,1)S(1)}, bf16[2,5,32,16]{3,2,0,1:T(8,128)(2,1)S(1)}, u32[]{:S(2)}, u32[]{:S(2)}) collective-permute-start(bf16[2,5,32,16]{3,2,0,1:T(8,128)(2,1)S(1)} %get-tuple-element.163), channel_id=1, source_target_pairs={{64,0},{128,64},{192,128},{65,1},{129,65},{193,129},{66,2},{130,66... | collective-permute-start | bytes 30728 | tf_op jit(solution)/shard_map/ppermute | solution.py:19
  172.3 8.2 %collective-permute-start.6 = (bf16[2,5,16,160]{3,2,0,1:T(8,128)(2,1)S(1)}, bf16[2,5,16,160]{3,2,0,1:T(8,128)(2,1)S(1)}, u32[]{:S(2)}, u32[]{:S(2)}) collective-permute-start(bf16[2,5,16,160]{3,2,0,1:T(8,128)(2,1)S(1)} %get-tuple-element.159), channel_id=1, source_target_pairs={{0,1},{1,2},{2,3},{3,4},{4,5},{5,6},{6,7},{7,8},{8,9},{9,10},{10,1... | collective-permute-start | bytes 153608 | tf_op jit(solution)/shard_map/ppermute | solution.py:16
  177.3 9.7 %collective-permute-start.7 = (bf16[2,5,16,160]{3,2,0,1:T(8,128)(2,1)S(1)}, bf16[2,5,16,160]{3,2,0,1:T(8,128)(2,1)S(1)}, u32[]{:S(2)}, u32[]{:S(2)}) collective-permute-start(bf16[2,5,16,160]{3,2,0,1:T(8,128)(2,1)S(1)} %get-tuple-element.158), channel_id=1, source_target_pairs={{1,0},{2,1},{3,2},{4,3},{5,4},{6,5},{7,6},{8,7},{9,8},{10,9},{11,1... | collective-permute-start | bytes 153608 | tf_op jit(solution)/shard_map/ppermute | solution.py:19
  189.0 13.6 %copy-start.2 = (f32[16,32,512]{2,1,0:T(8,128)S(1)}, f32[16,32,512]{2,1,0:T(8,128)}, u32[]{:S(2)}) copy-start(f32[16,32,512]{2,1,0:T(8,128)} %param.12) | copy-start | bytes 3145732
  189.0 13.6 %copy-start.7 = (f32[16]{0:T(128)S(1)}, f32[16]{0:T(128)}, u32[]{:S(2)}) copy-start(f32[16]{0:T(128)} %param.13) | copy-start | bytes 196
Sparse Core Ops, SparseCore 0:
  10.7 23.4 reduce-scatter.1
